TPU v7x, 128 devices: a whole 4x4x4 slice. The times are simulated.
128 devices in a mesh: chan: 32 (over y, z, x_lo), tm: 4 (over x_hi, core).
Axes of the slice: x: 4 (x_hi: 2, x_lo: 2; x = x_hi * 2 + x_lo), y: 4, z: 4, core: 2. Of those that a mesh axis runs over, the one named last changes fastest.
Arguments:
- record: float32 [64, 256, 16384], P('tm', 'chan'), may hold values from -6 to 6
- fir_taps: float32 [64], replicated, may hold values from -0.75 to 0.75
- pair_offsets: int32 [8], replicated, may hold values from -128 to 128, as said below
Outputs:
- correlation: float32 [8, 256, 16384], P('tm', None, 'chan')
Inputs may be any that keep to these rules, and one draw needn't show every extreme that they name: `pair_offsets`: 8 distinct nonzero channel offsets; both -128 and 128 are among them.
All inputs are finite; a program needn't handle non-finite values.
Results may differ from a plain program's by a relative error of at most 0.000098.
Values sent between devices are 32-bit elements; how exact they have to be, the bound alone decides.
No kernel may reach another device: no remote copies, remote signals or barrier semaphores. Data moves between devices by JAX's collectives and lax.ppermute only.
A program may use at most 192 MiB of HBM per device.

v0:
```python
import math

import jax
import jax.numpy as jnp
from jax import lax
from jax.experimental import pallas as pl
from jax.experimental.pallas import tpu as pltpu
from jax.sharding import PartitionSpec as P

S = 256
R = 128


PRECISE = lax.Precision.HIGHEST
FAST = lax.Precision.HIGH


def fir_matrix_of(fir_taps, seg_len):
    row_ids = lax.broadcasted_iota(jnp.int32, (seg_len, seg_len), 0)
    col_ids = lax.broadcasted_iota(jnp.int32, (seg_len, seg_len), 1)
    spread = col_ids - row_ids
    tap_ids = lax.broadcasted_iota(jnp.int32, (1, 1, fir_taps.shape[0]), 2)
    hits = spread[:, :, None] == tap_ids
    return jnp.sum(jnp.where(hits, fir_taps[None, None, :], 0.0), axis=2)


def forward_table(seg_len):
    length = 2 * seg_len
    time_ids = lax.broadcasted_iota(jnp.int32, (seg_len, length), 0)
    slot_ids = lax.broadcasted_iota(jnp.int32, (seg_len, length), 1)
    frequency = jnp.where(slot_ids <= seg_len, slot_ids, slot_ids - seg_len)
    angles = (frequency * time_ids % length).astype(jnp.float32) * (2.0 * math.pi / length)
    return jnp.where(slot_ids <= seg_len, jnp.cos(angles), jnp.sin(angles))


def inverse_table(seg_len, norm_scale):
    length = 2 * seg_len
    slot_ids = lax.broadcasted_iota(jnp.int32, (3 * seg_len, seg_len), 0)
    lag_ids = lax.broadcasted_iota(jnp.int32, (3 * seg_len, seg_len), 1) - seg_len // 2
    cosine_rows = slot_ids < length
    frequency = jnp.where(
        cosine_rows, jnp.where(slot_ids <= seg_len, slot_ids, slot_ids - seg_len), slot_ids - length
    )
    angles = (frequency * lag_ids % length).astype(jnp.float32) * (2.0 * math.pi / length)
    edge_rows = (slot_ids == 0) | (slot_ids == seg_len)
    cosine_weights = jnp.where(edge_rows, 1.0 / length, 2.0 / length)
    sine_weights = jnp.where(frequency == 0, 0.0, -2.0 / length)
    values = jnp.where(
        cosine_rows, cosine_weights * jnp.cos(angles), sine_weights * jnp.sin(angles)
    )
    return values * norm_scale


def halo(array, axis, dim, width):
    size, length = (lax.axis_size(axis), array.shape[dim])
    up = [(i, (i + 1) % size) for i in range(size)]
    down = [(j, i) for i, j in up]
    last = lax.slice_in_dim(array, length - width, length, axis=dim)
    first = lax.slice_in_dim(array, 0, width, axis=dim)
    before = lax.ppermute(last, axis, up)
    after = lax.ppermute(first, axis, down)
    return jnp.concatenate([before, array, after], axis=dim)


CHUNKS = 4


def cross_kernel(offs_ref, *refs):
    spec_refs, acc_ref, out_ref = refs[:-2], refs[-2], refs[-1]
    ext, width = spec_refs[0].shape[1:]
    half = width // 2
    start = R + offs_ref[pl.program_id(0)]
    rem = start % 8
    base = start - rem
    turn = (8 - rem) % 8
    keep = lax.broadcasted_iota(jnp.int32, (8, width), 0) < 8 - rem
    first = lax.broadcasted_iota(jnp.int32, (8, half), 1) == 0

    def body(r, carry):
        r0 = pl.multiple_of(R + r * 16, 8)
        p0 = pl.multiple_of(base + r * 16, 8)
        p2 = pl.multiple_of(jnp.minimum(p0 + 16, ext - 8), 8)
        o0 = pl.multiple_of(r * 16, 8)
        acc_m = [jnp.zeros((8, width), jnp.float32) for h in range(2)]
        acc_hi = [jnp.zeros((8, half), jnp.float32) for h in range(2)]
        acc_lo = [jnp.zeros((8, half), jnp.float32) for h in range(2)]
        for spec_ref, s in [(f, s) for f in spec_refs for s in range(f.shape[0])]:
            c0 = pltpu.roll(spec_ref[s, pl.ds(p0, 8), :], turn, 0)
            c1 = pltpu.roll(spec_ref[s, pl.ds(p0 + 8, 8), :], turn, 0)
            c2 = pltpu.roll(spec_ref[s, pl.ds(p2, 8), :], turn, 0)
            partners = (jnp.where(keep, c0, c1), jnp.where(keep, c1, c2))
            for h in range(2):
                a = spec_ref[s, pl.ds(r0 + 8 * h, 8), :]
                b = partners[h]
                acc_m[h] = acc_m[h] + a * b
                acc_lo[h] = acc_lo[h] + a[:, :half] * b[:, half:]
                acc_hi[h] = acc_hi[h] + a[:, half:] * b[:, :half]
        for h in range(2):
            rows = pl.ds(o0 + 8 * h, 8)
            cos_part = acc_m[h][:, :half]
            sin_part = acc_m[h][:, half:]
            skew = acc_hi[h] - acc_lo[h]
            out_ref[rows, 0:half] = acc_ref[rows, 0:half] + cos_part + jnp.where(first, 0.0, sin_part)
            out_ref[rows, half:] = acc_ref[rows, half:] + jnp.where(first, sin_part, skew)
        return carry

    lax.fori_loop(0, (ext - 2 * R) // 16, body, 0)


def cross_spectra(spectra_list, offsets, acc):
    n_k, own_w, out_w = acc.shape
    spec_specs = [
        pl.BlockSpec(f.shape, lambda k, offs: (0, 0, 0), pipeline_mode=pl.Buffered(1))
        for f in spectra_list
    ]
    grid_spec = pltpu.PrefetchScalarGridSpec(
        num_scalar_prefetch=1,
        grid=(n_k,),
        in_specs=spec_specs + [pl.BlockSpec((None, own_w, out_w), lambda k, offs: (k, 0, 0))],
        out_specs=pl.BlockSpec((None, own_w, out_w), lambda k, offs: (k, 0, 0)),
    )
    return pl.pallas_call(
        cross_kernel,
        grid_spec=grid_spec,
        out_shape=jax.ShapeDtypeStruct(acc.shape, jnp.float32),
        input_output_aliases={1 + len(spectra_list): 0},
        compiler_params=pltpu.CompilerParams(
            dimension_semantics=("arbitrary",), vmem_limit_bytes=48 * 1024 * 1024
        ),
    )(offsets, *spectra_list, acc)


def windows(piece, n_chan, width):
    segs, rows, channels = piece.shape
    blocks = piece.reshape(segs, rows, n_chan, channels // n_chan)
    before = jnp.roll(blocks, 1, axis=2)[..., -width:]
    after = jnp.roll(blocks, -1, axis=2)[..., :width]
    return jnp.concatenate([before, blocks, after], axis=3).transpose(2, 0, 1, 3)


def per_device(record, fir_taps, pair_offsets):
    n_chan = lax.axis_size("chan")
    n_time = lax.axis_size("tm")
    seg_count, part_rows, channels = record.shape
    block_width = channels // n_chan
    table = jnp.dot(fir_matrix_of(fir_taps, S), forward_table(S), precision=PRECISE)
    table = table.reshape(n_chan, part_rows, 2 * S)
    norm_scale = 1.0 / math.sqrt(seg_count * n_time * S)
    inverse = inverse_table(S, norm_scale)
    inverse_cat = jnp.concatenate([inverse[: S + 1], inverse[2 * S + 1 :]], axis=0)
    even_offsets = pair_offsets[0::2]
    odd_offsets = pair_offsets[1::2]
    acc_shape = (even_offsets.shape[0], block_width, 2 * S)
    even = jnp.zeros(acc_shape, jnp.float32)
    odd = jnp.zeros(acc_shape, jnp.float32)
    step = seg_count // CHUNKS
    edge = step // 2

    def build(first, size):
        return windows(lax.dynamic_slice_in_dim(record, first, size, 0), n_chan, R)

    def send(piece):
        return lax.all_to_all(piece, "chan", split_axis=0, concat_axis=0, tiled=True)

    def spectra_of(turned):
        return jnp.einsum("asuc,auj->scj", turned, table, precision=FAST)

    def accumulate(turned, even, odd):
        spectra = [spectra_of(turned)]
        return cross_spectra(spectra, even_offsets, even), cross_spectra(spectra, odd_offsets, odd)

    def body(g, carry):
        turned, piece, even, odd = carry
        upcoming = send(piece)
        later = build(edge + (g + 2) * step, step)
        even, odd = accumulate(turned, even, odd)
        return upcoming, later, even, odd

    opening = send(build(0, edge))
    turned = send(build(edge, step))
    piece = build(edge + step, step)
    even, odd = accumulate(opening, even, odd)
    carry = (turned, piece, even, odd)
    turned, piece, even, odd = lax.fori_loop(0, CHUNKS - 2, body, carry)
    held, turned = lax.optimization_barrier((build(seg_count - edge, edge), turned))
    closing = send(held)
    last_full = spectra_of(turned)
    even = cross_spectra([last_full], even_offsets, even)
    last_small = spectra_of(closing)
    even = cross_spectra([last_small], even_offsets, even)
    odd = cross_spectra([last_full, last_small], odd_offsets, odd)

    def finish(crossed):
        lagged = jnp.einsum("kcr,rl->klc", crossed, inverse_cat, precision=FAST)
        parts = lax.all_to_all(lagged, "tm", split_axis=0, concat_axis=0, tiled=True)
        return jnp.sum(parts, axis=0, keepdims=True)

    first = finish(even)
    second = finish(odd)
    return jnp.concatenate([first, second], axis=0)


def solution(mesh):
    placed = (P("tm", "chan", None), P(), P())
    return jax.shard_map(
        per_device, mesh=mesh, in_specs=placed, out_specs=P("tm", None, "chan"), check_vma=False
    )
```

profile of v0, /device:TPU:1, one launch (start us, length us, event | category | flops | bytes accessed | tf_op | source)
XLA Modules:
  0.0 313.2 jit_solution(9242068061505527824)
XLA Ops:
  0.0 1.8 fusion.52
  5.8 2.1 copy.38
  9.1 4.3 %select_multiply_fusion = f32[768,256]{0,1:T(8,128)} fusion(s32[256]{0:T(256)S(1)} %iota_add_fusion.3, s32[768]{0:T(1024)S(1)} %get-tuple-element.284, s32[768]{0:T(1024)S(1)} %get-tuple-element.285, f32[768]{0:T(1024)S(1)} %fusion.43, pred[768]{0:T(1024)(128)(4,1)S(1)} %get-tuple-element.286, pred[768]{0:T(1024)(128)(4,1)S(1)} %get-tuple-element.287), kind=kLoop, calls=%fused_computation.48 | loop fusion | flops 4325376 | bytes 798208 | tf_op jit(solution)/shard_map/mul | solution.py:51
  13.4 9.9 %all-to-all-start.2 = ((f32[32,2,8,768]{3,2,1,0:T(8,128)}), f32[32,2,8,768]{3,2,1,0:T(8,128)}, u32[]{:S(2)}, u32[]{:S(2)}) async-start(f32[32,2,8,768]{3,2,1,0:T(8,128)} %copy.38), calls=%async_computation.2 | async-start | bytes 3145728 | tf_op jit(solution)/shard_map/all_to_all | solution.py:163
  23.6 1.8 slice.184
  25.4 1.8 slice.185
  28.1 3.5 %copy.37 = f32[32,4,8,768]{3,2,1,0:T(8,128)} copy(f32[32,4,8,768]{3,0,2,1:T(8,128)S(1)} %fusion.8) | data formatting | bytes 6291456 | tf_op jit(solution)/shard_map/transpose | solution.py:138
  32.5 15.1 %all-to-all-done.2 = f32[32,2,8,768]{3,2,1,0:T(8,128)} async-done(((f32[32,2,8,768]{3,2,1,0:T(8,128)}), f32[32,2,8,768]{3,2,1,0:T(8,128)}, u32[]{:S(2)}, u32[]{:S(2)}) %all-to-all-start.2) | async-done | bytes 1572896 | tf_op jit(solution)/shard_map/all_to_all | solution.py:163
  47.6 5.0 %all-to-all-start.1 = ((f32[32,4,8,768]{3,2,1,0:T(8,128)}), f32[32,4,8,768]{3,2,1,0:T(8,128)}, u32[]{:S(2)}, u32[]{:S(2)}) async-start(f32[32,4,8,768]{3,2,1,0:T(8,128)} %copy.37), calls=%async_computation.1 | async-start | bytes 6291456 | tf_op jit(solution)/shard_map/all_to_all | solution.py:163
  55.4 1.9 fusion.5
  57.3 5.7 %select_reduce_fusion = f32[256,256]{1,0:T(8,128)S(1)} fusion(f32[64]{0:T(128)S(1)} %copy-done.9, s32[256,256]{1,0:T(8,128)S(1)} %iota_subtract_fusion), kind=kLoop, calls=%fused_computation.8 | loop fusion | flops 12517376 | bytes 524544 | tf_op jit(solution)/shard_map/reduce_sum | solution.py:24
  63.0 3.0 fusion.26
  66.1 3.0 convolution_bitcast_fusion.3.refs_0_
  69.1 2.6 broadcast_9_refs_1_.2.clone.refs_1_
  71.7 6.7 %shard_map.37 = f32[4,512,512]{2,1,0:T(8,128)} custom-call(s32[4]{0:T(128)S(1)} %slice.154.offs_ref, f32[2,768,512]{2,1,0:T(8,128)S(1)} %convolution_bitcast_fusion.3.refs_0_, f32[4,512,512]{2,1,0:T(8,128)} %broadcast_9_refs_1_.2.clone.refs_1_), custom_call_target="tpu_custom_call", output_to_operand_aliasing={{}: (2, {})} | custom-call | tf_op jit(solution)/shard_map/pallas_call | solution.py:122
  78.4 2.6 broadcast_9_refs_1_.2.clone.1.refs_1_
  80.9 6.6 %shard_map.38 = f32[4,512,512]{2,1,0:T(8,128)} custom-call(s32[4]{0:T(128)S(1)} %slice.179.offs_ref, f32[2,768,512]{2,1,0:T(8,128)S(1)} %convolution_bitcast_fusion.3.refs_0_, f32[4,512,512]{2,1,0:T(8,128)} %broadcast_9_refs_1_.2.clone.1.refs_1_), custom_call_target="tpu_custom_call", output_to_operand_aliasing={{}: (2, {})} | custom-call | tf_op jit(solution)/shard_map/pallas_call | solution.py:122
  87.6 9.6 %all-to-all-done.1 = f32[32,4,8,768]{3,2,1,0:T(8,128)} async-done(((f32[32,4,8,768]{3,2,1,0:T(8,128)}), f32[32,4,8,768]{3,2,1,0:T(8,128)}, u32[]{:S(2)}, u32[]{:S(2)}) %all-to-all-start.1) | async-done | bytes 3145760 | tf_op jit(solution)/shard_map/all_to_all | solution.py:163
  97.1 103.9 %while.21 = (s32[]{:T(128)}, f32[32,4,8,768]{3,2,1,0:T(8,128)}, f32[32,4,8,768]{3,2,0,1:T(8,128)}, f32[4,512,512]{2,1,0:T(8,128)}, f32[4,512,512]{2,1,0:T(8,128)...) while((s32[]{:T(128)}, f32[32,4,8,768]{3,2,1,0:T(8,128)}, ...), condition=%wide.region_2.3_spmd, body=%wide.region_1.2_spmd.sunk | while | flops 2419064832 | bytes 54001900 | solution.py:184
  97.1 3.9 %copy.52 = f32[32,4,8,768]{3,2,1,0:T(8,128)} copy(f32[32,4,8,768]{3,2,0,1:T(8,128)} %get-tuple-element.367) | data formatting | bytes 6291456 | tf_op jit(solution)/shard_map
  101.1 4.1 %all-to-all-start = ((f32[32,4,8,768]{3,2,1,0:T(8,128)}), f32[32,4,8,768]{3,2,1,0:T(8,128)S(1)}, u32[]{:S(2)}, u32[]{:S(2)}) async-start(f32[32,4,8,768]{3,2,1,0:T(8,128)} %copy.52), calls=%async_computation | async-start | bytes 6291456 | tf_op jit(solution)/shard_map/while/body/eval_jaxpr/all_to_all | solution.py:163
  105.1 7.3 %convolution_bitcast_fusion.7.refs_0_ = f32[4,768,512]{2,1,0:T(8,128)} fusion(f32[32,4,8,768]{3,2,1,0:T(8,128)} %get-tuple-element.366, f32[32,8,512]{2,1,0:T(8,128)} %get-tuple-element.385), kind=kOutput, calls=%fused_computation.5.clone.1 | convolution fusion | flops 2415919104 | bytes 9961472 | tf_op jit(solution)/shard_map/while/body/eval_jaxpr/asuc,auj->scj/dot_general | solution.py:166
  112.4 9.9 %eval_jaxpr.16 = f32[4,512,512]{2,1,0:T(8,128)} custom-call(s32[4]{0:T(128)S(1)} %get-tuple-element.386.offs_ref, f32[4,768,512]{2,1,0:T(8,128)} %convolution_bitcast_fusion.7.refs_0_, f32[4,512,512]{2,1,0:T(8,128)} %get-tuple-element.368.refs_1_), custom_call_target="tpu_custom_call", output_to_operand_aliasing={{}: (2, {})} | custom-call | tf_op jit(solution)/shard_map/while/body/eval_jaxpr/pallas_call | solution.py:122
  122.4 9.9 %eval_jaxpr.17 = f32[4,512,512]{2,1,0:T(8,128)} custom-call(s32[4]{0:T(128)S(1)} %get-tuple-element.387.offs_ref, f32[4,768,512]{2,1,0:T(8,128)} %convolution_bitcast_fusion.7.refs_0_, f32[4,512,512]{2,1,0:T(8,128)} %get-tuple-element.369.refs_1_), custom_call_target="tpu_custom_call", output_to_operand_aliasing={{}: (2, {})} | custom-call | tf_op jit(solution)/shard_map/while/body/eval_jaxpr/pallas_call | solution.py:122
  134.6 1.9 fusion.77
  136.5 11.1 %all-to-all-done = f32[32,4,8,768]{3,2,1,0:T(8,128)S(1)} async-done(((f32[32,4,8,768]{3,2,1,0:T(8,128)}), f32[32,4,8,768]{3,2,1,0:T(8,128)S(1)}, u32[]{:S(2)}, u32[]{:S(2)}) %all-to-all-start) | async-done | bytes 3145760 | tf_op jit(solution)/shard_map/while/body/eval_jaxpr/all_to_all | solution.py:163
  149.2 3.9 %copy.52 = f32[32,4,8,768]{3,2,1,0:T(8,128)} copy(f32[32,4,8,768]{3,2,0,1:T(8,128)} %get-tuple-element.367) | data formatting | bytes 6291456 | tf_op jit(solution)/shard_map
  153.1 4.4 %all-to-all-start = ((f32[32,4,8,768]{3,2,1,0:T(8,128)}), f32[32,4,8,768]{3,2,1,0:T(8,128)S(1)}, u32[]{:S(2)}, u32[]{:S(2)}) async-start(f32[32,4,8,768]{3,2,1,0:T(8,128)} %copy.52), calls=%async_computation | async-start | bytes 6291456 | tf_op jit(solution)/shard_map/while/body/eval_jaxpr/all_to_all | solution.py:163
  157.6 7.3 %convolution_bitcast_fusion.7.refs_0_ = f32[4,768,512]{2,1,0:T(8,128)} fusion(f32[32,4,8,768]{3,2,1,0:T(8,128)} %get-tuple-element.366, f32[32,8,512]{2,1,0:T(8,128)} %get-tuple-element.385), kind=kOutput, calls=%fused_computation.5.clone.1 | convolution fusion | flops 2415919104 | bytes 9961472 | tf_op jit(solution)/shard_map/while/body/eval_jaxpr/asuc,auj->scj/dot_general | solution.py:166
  164.9 9.9 %eval_jaxpr.16 = f32[4,512,512]{2,1,0:T(8,128)} custom-call(s32[4]{0:T(128)S(1)} %get-tuple-element.386.offs_ref, f32[4,768,512]{2,1,0:T(8,128)} %convolution_bitcast_fusion.7.refs_0_, f32[4,512,512]{2,1,0:T(8,128)} %get-tuple-element.368.refs_1_), custom_call_target="tpu_custom_call", output_to_operand_aliasing={{}: (2, {})} | custom-call | tf_op jit(solution)/shard_map/while/body/eval_jaxpr/pallas_call | solution.py:122
  174.8 9.9 %eval_jaxpr.17 = f32[4,512,512]{2,1,0:T(8,128)} custom-call(s32[4]{0:T(128)S(1)} %get-tuple-element.387.offs_ref, f32[4,768,512]{2,1,0:T(8,128)} %convolution_bitcast_fusion.7.refs_0_, f32[4,512,512]{2,1,0:T(8,128)} %get-tuple-element.369.refs_1_), custom_call_target="tpu_custom_call", output_to_operand_aliasing={{}: (2, {})} | custom-call | tf_op jit(solution)/shard_map/while/body/eval_jaxpr/pallas_call | solution.py:122
  187.1 1.9 fusion.77
  188.9 10.4 %all-to-all-done = f32[32,4,8,768]{3,2,1,0:T(8,128)S(1)} async-done(((f32[32,4,8,768]{3,2,1,0:T(8,128)}), f32[32,4,8,768]{3,2,1,0:T(8,128)S(1)}, u32[]{:S(2)}, u32[]{:S(2)}) %all-to-all-start) | async-done | bytes 3145760 | tf_op jit(solution)/shard_map/while/body/eval_jaxpr/all_to_all | solution.py:163
  201.0 3.5 %copy.39 = f32[32,2,8,768]{3,2,1,0:T(8,128)} copy(f32[32,2,8,768]{3,0,2,1:T(8,128)} %fusion.14) | data formatting | bytes 3145728 | tf_op jit(solution)/shard_map/optimization_barrier | solution.py:185
  204.5 5.4 %all-to-all-start.3 = ((f32[32,2,8,768]{3,2,1,0:T(8,128)}), f32[32,2,8,768]{3,2,1,0:T(8,128)}, u32[]{:S(2)}, u32[]{:S(2)}) async-start(f32[32,2,8,768]{3,2,1,0:T(8,128)} %copy.39), calls=%async_computation.3 | async-start | bytes 3145728 | tf_op jit(solution)/shard_map/all_to_all | solution.py:163
  210.0 9.0 %convolution_bitcast_fusion.1.refs_0_ = f32[4,768,512]{2,1,0:T(8,128)} fusion(f32[32,4,8,768]{3,2,1,0:T(8,128)} %get-tuple-element.221, f32[32,8,512]{2,1,0:T(8,128)S(1)} %copy-done.12), kind=kOutput, calls=%fused_computation.20 | convolution fusion | flops 2415919104 | bytes 9961472 | tf_op jit(solution)/shard_map/asuc,auj->scj/dot_general | solution.py:166
  218.9 9.9 %shard_map.39.refs_1_ = f32[4,512,512]{2,1,0:T(8,128)} custom-call(s32[4]{0:T(128)S(1)} %get-tuple-element.403, f32[4,768,512]{2,1,0:T(8,128)} %convolution_bitcast_fusion.1.refs_0_, f32[4,512,512]{2,1,0:T(8,128)} %get-tuple-element.222.refs_1_), custom_call_target="tpu_custom_call", output_to_operand_aliasing={{}: (2, {})} | custom-call | tf_op jit(solution)/shard_map/pallas_call | solution.py:122
  228.9 2.7 all-to-all-done.3
  231.6 2.9 convolution_bitcast_fusion.2.refs_0_.refs_1_
  234.6 6.7 %shard_map.40 = f32[4,512,512]{2,1,0:T(8,128)} custom-call(s32[4]{0:T(128)S(1)} %copy-done.6, f32[2,768,512]{2,1,0:T(8,128)S(1)} %convolution_bitcast_fusion.2.refs_0_.refs_1_, f32[4,512,512]{2,1,0:T(8,128)} %shard_map.39.refs_1_), custom_call_target="tpu_custom_call", output_to_operand_aliasing={{}: (2, {})} | custom-call | tf_op jit(solution)/shard_map/pallas_call | solution.py:122
  241.2 5.4 %convolution_bitcast_fusion.5 = f32[4,256,512]{2,1,0:T(8,128)} fusion(f32[4,512,512]{2,1,0:T(8,128)} %shard_map.40, f32[255,256]{0,1:T(8,128)S(1)} %copy-done.3, f32[257,256]{0,1:T(8,128)S(1)} %copy-done.2), kind=kOutput, calls=%fused_computation.25 | convolution fusion | flops 1610743808 | bytes 6815744 | tf_op jit(solution)/shard_map/kcr,rl->klc/dot_general | solution.py:194
  246.6 8.2 %all-to-all-start.4 = ((f32[4,256,512]{2,1,0:T(8,128)}), f32[4,256,512]{2,1,0:T(8,128)}, u32[]{:S(2)}, u32[]{:S(2)}) async-start(f32[4,256,512]{2,1,0:T(8,128)} %convolution_bitcast_fusion.5), calls=%async_computation.4 | async-start | bytes 4194304 | tf_op jit(solution)/shard_map/all_to_all | solution.py:195
  254.8 11.6 %shard_map.41 = f32[4,512,512]{2,1,0:T(8,128)} custom-call(s32[4]{0:T(128)S(1)} %copy-done.8, f32[4,768,512]{2,1,0:T(8,128)} %convolution_bitcast_fusion.1.refs_0_, f32[2,768,512]{2,1,0:T(8,128)S(1)} %convolution_bitcast_fusion.2.refs_0_.refs_1_, f32[4,512,512]{2,1,0:T(8,128)} %get-tuple-element.223.refs_2_), custom_call_target="tpu_custom_call", output_to_operand_aliasing={{}: (3, {})} | custom-call | tf_op jit(solution)/shard_map/pallas_call | solution.py:122
  266.5 5.4 %convolution_bitcast_fusion.4 = f32[4,256,512]{2,1,0:T(8,128)} fusion(f32[4,512,512]{2,1,0:T(8,128)} %shard_map.41, f32[255,256]{0,1:T(8,128)S(1)} %copy-done.4, f32[257,256]{0,1:T(8,128)S(1)} %copy-done.2), kind=kOutput, calls=%fused_computation.24 | convolution fusion | flops 1610743808 | bytes 6815744 | tf_op jit(solution)/shard_map/kcr,rl->klc/dot_general | solution.py:194
  271.9 9.2 %all-to-all-done.4 = f32[4,256,512]{2,1,0:T(8,128)} async-done(((f32[4,256,512]{2,1,0:T(8,128)}), f32[4,256,512]{2,1,0:T(8,128)}, u32[]{:S(2)}, u32[]{:S(2)}) %all-to-all-start.4) | async-done | bytes 2097184 | tf_op jit(solution)/shard_map/all_to_all | solution.py:195
  281.1 4.5 %all-to-all-start.5 = ((f32[4,256,512]{2,1,0:T(8,128)}), f32[4,256,512]{2,1,0:T(8,128)S(1)}, u32[]{:S(2)}, u32[]{:S(2)}) async-start(f32[4,256,512]{2,1,0:T(8,128)} %convolution_bitcast_fusion.4), calls=%async_computation.5 | async-start | bytes 4194304 | tf_op jit(solution)/shard_map/all_to_all | solution.py:195
  285.7 1.9 reduce_sum.28
  287.5 24.3 %all-to-all-done.5 = f32[4,256,512]{2,1,0:T(8,128)S(1)} async-done(((f32[4,256,512]{2,1,0:T(8,128)}), f32[4,256,512]{2,1,0:T(8,128)S(1)}, u32[]{:S(2)}, u32[]{:S(2)}) %all-to-all-start.5) | async-done | bytes 2097184 | tf_op jit(solution)/shard_map/all_to_all | solution.py:195
  (60 shorter events, 19.2 us)
Async XLA Ops:
  0.0 4.0 %copy-start = (f32[16,8,16384]{2,1,0:T(8,128)S(1)}, f32[16,8,16384]{2,1,0:T(8,128)}, u32[]{:S(2)}) copy-start(f32[16,8,16384]{2,1,0:T(8,128)} %param.5) | copy-start | bytes 25165828
  9.1 14.3 %copy-start.10 = (s32[8]{0:T(128)S(1)}, s32[8]{0:T(128)}, u32[]{:S(2)}) copy-start(s32[8]{0:T(128)} %param.7) | copy-start | bytes 100
  13.4 34.3 %all-to-all-start.2 = ((f32[32,2,8,768]{3,2,1,0:T(8,128)}), f32[32,2,8,768]{3,2,1,0:T(8,128)}, u32[]{:S(2)}, u32[]{:S(2)}) async-start(f32[32,2,8,768]{3,2,1,0:T(8,128)} %copy.38), calls=%async_computation.2 | async-start | bytes 3145728 | tf_op jit(solution)/shard_map/all_to_all | solution.py:163
  47.6 49.5 %all-to-all-start.1 = ((f32[32,4,8,768]{3,2,1,0:T(8,128)}), f32[32,4,8,768]{3,2,1,0:T(8,128)}, u32[]{:S(2)}, u32[]{:S(2)}) async-start(f32[32,4,8,768]{3,2,1,0:T(8,128)} %copy.37), calls=%async_computation.1 | async-start | bytes 6291456 | tf_op jit(solution)/shard_map/all_to_all | solution.py:163
  52.6 2.2 copy-start.1
  55.4 1.9 copy-start.9
  66.0 3.0 copy-start.11
  101.1 46.5 %all-to-all-start = ((f32[32,4,8,768]{3,2,1,0:T(8,128)}), f32[32,4,8,768]{3,2,1,0:T(8,128)S(1)}, u32[]{:S(2)}, u32[]{:S(2)}) async-start(f32[32,4,8,768]{3,2,1,0:T(8,128)} %copy.52), calls=%async_computation | async-start | bytes 6291456 | tf_op jit(solution)/shard_map/while/body/eval_jaxpr/all_to_all | solution.py:163
  153.1 46.2 %all-to-all-start = ((f32[32,4,8,768]{3,2,1,0:T(8,128)}), f32[32,4,8,768]{3,2,1,0:T(8,128)S(1)}, u32[]{:S(2)}, u32[]{:S(2)}) async-start(f32[32,4,8,768]{3,2,1,0:T(8,128)} %copy.52), calls=%async_computation | async-start | bytes 6291456 | tf_op jit(solution)/shard_map/while/body/eval_jaxpr/all_to_all | solution.py:163
  201.0 3.5 %copy-start.7 = (s32[4]{0:T(128)}, s32[4]{0:T(128)S(1)}, u32[]{:S(2)}) copy-start(s32[4]{0:T(128)S(1)} %get-tuple-element.404) | copy-start | bytes 52
  201.0 17.9 %copy-start.5 = (s32[4]{0:T(128)}, s32[4]{0:T(128)S(1)}, u32[]{:S(2)}) copy-start(s32[4]{0:T(128)S(1)} %get-tuple-element.403) | copy-start | bytes 52
  201.0 9.0 %copy-start.12 = (f32[32,8,512]{2,1,0:T(8,128)S(1)}, f32[32,8,512]{2,1,0:T(8,128)}, u32[]{:S(2)}) copy-start(f32[32,8,512]{2,1,0:T(8,128)} %get-tuple-element.405) | copy-start | bytes 1572868
  204.5 27.1 %all-to-all-start.3 = ((f32[32,2,8,768]{3,2,1,0:T(8,128)}), f32[32,2,8,768]{3,2,1,0:T(8,128)}, u32[]{:S(2)}, u32[]{:S(2)}) async-start(f32[32,2,8,768]{3,2,1,0:T(8,128)} %copy.39), calls=%async_computation.3 | async-start | bytes 3145728 | tf_op jit(solution)/shard_map/all_to_all | solution.py:163
  228.9 5.7 %copy-start.6 = (s32[4]{0:T(128)S(1)}, s32[4]{0:T(128)}, u32[]{:S(2)}) copy-start(s32[4]{0:T(128)} %copy-done.5) | copy-start | bytes 52
  234.5 6.7 %copy-start.2 = (f32[257,256]{0,1:T(8,128)S(1)}, f32[257,256]{0,1:T(8,128)}, u32[]{:S(2)}) copy-start(f32[257,256]{0,1:T(8,128)} %slice.184) | copy-start | bytes 789508
  234.5 6.7 %copy-start.3 = (f32[255,256]{0,1:T(8,128)S(1)}, f32[255,256]{0,1:T(8,128)}, u32[]{:S(2)}) copy-start(f32[255,256]{0,1:T(8,128)} %slice.185) | copy-start | bytes 783364
  246.6 8.2 %copy-start.8 = (s32[4]{0:T(128)S(1)}, s32[4]{0:T(128)}, u32[]{:S(2)}) copy-start(s32[4]{0:T(128)} %copy-done.7) | copy-start | bytes 52
  246.6 34.5 %all-to-all-start.4 = ((f32[4,256,512]{2,1,0:T(8,128)}), f32[4,256,512]{2,1,0:T(8,128)}, u32[]{:S(2)}, u32[]{:S(2)}) async-start(f32[4,256,512]{2,1,0:T(8,128)} %convolution_bitcast_fusion.5), calls=%async_computation.4 | async-start | bytes 4194304 | tf_op jit(solution)/shard_map/all_to_all | solution.py:195
  254.8 11.6 %copy-start.4 = (f32[255,256]{0,1:T(8,128)S(1)}, f32[255,256]{0,1:T(8,128)}, u32[]{:S(2)}) copy-start(f32[255,256]{0,1:T(8,128)} %slice.185) | copy-start | bytes 783364
  281.1 30.8 %all-to-all-start.5 = ((f32[4,256,512]{2,1,0:T(8,128)}), f32[4,256,512]{2,1,0:T(8,128)S(1)}, u32[]{:S(2)}, u32[]{:S(2)}) async-start(f32[4,256,512]{2,1,0:T(8,128)} %convolution_bitcast_fusion.4), calls=%async_computation.5 | async-start | bytes 4194304 | tf_op jit(solution)/shard_map/all_to_all | solution.py:195
where the time goes:
time: 315 us; the launch traced here: 313 us
  waiting for transfers between devices  82.4 us (26%)
  Pallas kernels  81.3 us (26%)
  local copies, waits for them, and re-layouts  43.6 us (14%)
  matrix products  43.3 us (14%)
  starting transfers between devices  41.6 us (13%)
  other arithmetic  20.6 us (7%)
    pallas_call x9, Pallas kernels, cross_spectra(): pl.pallas_call(cross_kernel, grid_spec=grid_spec, out_shape=jax.ShapeDtyp...  81.3 us
    all_to_all x5, waiting for transfers between devices, send(): lax.all_to_all(piece, 'chan', split_axis=0, concat_axis=0, tiled=True)  48.8 us
    all_to_all x2, waiting for transfers between devices, finish(): lax.all_to_all(lagged, 'tm', split_axis=0, concat_axis=0, tiled=True)  33.6 us
    dot_general x5, matrix products, spectra_of(): return jnp.einsum('asuc,auj->scj', turned, table, precision=FAST)  29.5 us
    all_to_all x5, starting transfers between devices, send(): lax.all_to_all(piece, 'chan', split_axis=0, concat_axis=0, tiled=True)  28.8 us
    another operation x4, local copies, waits for them, and re-layouts  13 us
    all_to_all x2, starting transfers between devices, finish(): lax.all_to_all(lagged, 'tm', split_axis=0, concat_axis=0, tiled=True)  12.8 us
    dot_general x2, matrix products, finish(): lagged = jnp.einsum('kcr,rl->klc', crossed, inverse_cat, precision=FAST)  10.8 us
  transfers between devices with their start and end apart: 7, of which 7 were waited for; matrix products, arithmetic and copies ran while one was open for 22% of the time, Pallas kernels for 24%

commit v1 on v0

--- a/solution.py
+++ b/solution.py
@@ -190,13 +190,15 @@
     even = cross_spectra([last_small], even_offsets, even)
     odd = cross_spectra([last_full, last_small], odd_offsets, odd)
 
-    def finish(crossed):
+    def finish(crossed, offload):
         lagged = jnp.einsum("kcr,rl->klc", crossed, inverse_cat, precision=FAST)
+        if offload:
+            return lax.psum_scatter(lagged, "tm", scatter_dimension=0, tiled=True)
         parts = lax.all_to_all(lagged, "tm", split_axis=0, concat_axis=0, tiled=True)
         return jnp.sum(parts, axis=0, keepdims=True)
 
-    first = finish(even)
-    second = finish(odd)
+    first = finish(even, True)
+    second = finish(odd, False)
     return jnp.concatenate([first, second], axis=0)
 
 

time: 315 us -> 325 us (1.032)
  blocking collectives: 0 us -> 44.9 us
  waiting for transfers between devices: 82.4 us -> 48.6 us
  between operations: 0.28 us -> 13.7 us
  starting transfers between devices: 41.6 us -> 28.9 us
    all_to_all x0 -> x1, blocking collectives: none -> 44.9 us  [finish(): lax.all_to_all(lagged, 'tm', split_axis=0, concat_axis=0, tiled=True)]
    all_to_all x2 -> x0, waiting for transfers between devices: 33.6 us -> none  [finish(): lax.all_to_all(lagged, 'tm', split_axis=0, concat_axis=0, tiled=True)]
    all_to_all x2 -> x0, starting transfers between devices: 12.8 us -> none  [finish(): lax.all_to_all(lagged, 'tm', split_axis=0, concat_axis=0, tiled=True)]
  transfers between devices with their start and end apart: 7 -> 6, of which waited for: 7 -> 5; matrix products, arithmetic and copies ran while one was open for 22% -> 21% of each run, Pallas kernels for 24% -> 23%
where the time goes in v1:
time: 325 us; the launch traced here: 323 us
  Pallas kernels  81.2 us (25%)
  waiting for transfers between devices  48.6 us (15%)
  blocking collectives  44.9 us (14%)
  local copies, waits for them, and re-layouts  43.6 us (13%)
  matrix products  42.3 us (13%)
  starting transfers between devices  28.9 us (9%)
  other arithmetic  19.8 us (6%)
  between operations  13.7 us (4%)
    pallas_call x9, Pallas kernels, cross_spectra(): pl.pallas_call(cross_kernel, grid_spec=grid_spec, out_shape=jax.ShapeDtyp...  81.2 us
    all_to_all x5, waiting for transfers between devices, send(): lax.all_to_all(piece, 'chan', split_axis=0, concat_axis=0, tiled=True)  48.6 us
    all_to_all x1, blocking collectives, finish(): lax.all_to_all(lagged, 'tm', split_axis=0, concat_axis=0, tiled=True)  44.9 us
    dot_general x5, matrix products, spectra_of(): return jnp.einsum('asuc,auj->scj', turned, table, precision=FAST)  29.7 us
    all_to_all x5, starting transfers between devices, send(): lax.all_to_all(piece, 'chan', split_axis=0, concat_axis=0, tiled=True)  28.8 us
    another operation x4, local copies, waits for them, and re-layouts  13 us
    dot_general x2, matrix products, finish(): lagged = jnp.einsum('kcr,rl->klc', crossed, inverse_cat, precision=FAST)  9.57 us
    transpose x6, other arithmetic, windows(): jnp.concatenate([before, blocks, after], axis=3).transpose(2, 0, 1, 3)  7.42 us
  transfers between devices with their start and end apart: 6, of which 5 were waited for; matrix products, arithmetic and copies ran while one was open for 21% of the time, Pallas kernels for 23%

profile of v1, /device:TPU:1, one launch (start us, length us, event | category | flops | bytes accessed | tf_op | source)
XLA Modules:
  0.0 323.1 jit_solution(17804159374243780182)
XLA Ops:
  6.5 1.8 fusion.52
  12.3 2.1 copy.38
  15.6 4.3 %select_multiply_fusion = f32[768,256]{0,1:T(8,128)} fusion(s32[256]{0:T(256)S(1)} %iota_add_fusion.3, s32[768]{0:T(1024)S(1)} %get-tuple-element.284, s32[768]{0:T(1024)S(1)} %get-tuple-element.285, f32[768]{0:T(1024)S(1)} %fusion.43, pred[768]{0:T(1024)(128)(4,1)S(1)} %get-tuple-element.286, pred[768]{0:T(1024)(128)(4,1)S(1)} %get-tuple-element.287), kind=kLoop, calls=%fused_computation.48 | loop fusion | flops 4325376 | bytes 798208 | tf_op jit(solution)/shard_map/mul | solution.py:51
  19.9 9.9 %all-to-all-start.2 = ((f32[32,2,8,768]{3,2,1,0:T(8,128)}), f32[32,2,8,768]{3,2,1,0:T(8,128)}, u32[]{:S(2)}, u32[]{:S(2)}) async-start(f32[32,2,8,768]{3,2,1,0:T(8,128)} %copy.38), calls=%async_computation.2 | async-start | bytes 3145728 | tf_op jit(solution)/shard_map/all_to_all | solution.py:163
  30.1 1.8 slice.184
  31.9 1.8 slice.185
  34.6 3.5 %copy.37 = f32[32,4,8,768]{3,2,1,0:T(8,128)} copy(f32[32,4,8,768]{3,0,2,1:T(8,128)S(1)} %fusion.8) | data formatting | bytes 6291456 | tf_op jit(solution)/shard_map/transpose | solution.py:138
  39.1 15.1 %all-to-all-done.2 = f32[32,2,8,768]{3,2,1,0:T(8,128)} async-done(((f32[32,2,8,768]{3,2,1,0:T(8,128)}), f32[32,2,8,768]{3,2,1,0:T(8,128)}, u32[]{:S(2)}, u32[]{:S(2)}) %all-to-all-start.2) | async-done | bytes 1572896 | tf_op jit(solution)/shard_map/all_to_all | solution.py:163
  54.2 5.0 %all-to-all-start.1 = ((f32[32,4,8,768]{3,2,1,0:T(8,128)}), f32[32,4,8,768]{3,2,1,0:T(8,128)}, u32[]{:S(2)}, u32[]{:S(2)}) async-start(f32[32,4,8,768]{3,2,1,0:T(8,128)} %copy.37), calls=%async_computation.1 | async-start | bytes 6291456 | tf_op jit(solution)/shard_map/all_to_all | solution.py:163
  62.0 1.9 fusion.5
  63.8 5.7 %select_reduce_fusion = f32[256,256]{1,0:T(8,128)S(1)} fusion(f32[64]{0:T(128)S(1)} %copy-done.9, s32[256,256]{1,0:T(8,128)S(1)} %iota_subtract_fusion), kind=kLoop, calls=%fused_computation.8 | loop fusion | flops 12517376 | bytes 524544 | tf_op jit(solution)/shard_map/reduce_sum | solution.py:24
  69.5 3.0 fusion.26
  72.6 3.0 convolution_bitcast_fusion.3.refs_0_
  75.6 2.6 broadcast_9_refs_1_.2.clone.refs_1_
  78.2 6.7 %shard_map.37 = f32[4,512,512]{2,1,0:T(8,128)} custom-call(s32[4]{0:T(128)S(1)} %slice.154.offs_ref, f32[2,768,512]{2,1,0:T(8,128)S(1)} %convolution_bitcast_fusion.3.refs_0_, f32[4,512,512]{2,1,0:T(8,128)} %broadcast_9_refs_1_.2.clone.refs_1_), custom_call_target="tpu_custom_call", output_to_operand_aliasing={{}: (2, {})} | custom-call | tf_op jit(solution)/shard_map/pallas_call | solution.py:122
  84.9 2.6 broadcast_9_refs_1_.2.clone.1.refs_1_
  87.5 6.6 %shard_map.38 = f32[4,512,512]{2,1,0:T(8,128)} custom-call(s32[4]{0:T(128)S(1)} %slice.179.offs_ref, f32[2,768,512]{2,1,0:T(8,128)S(1)} %convolution_bitcast_fusion.3.refs_0_, f32[4,512,512]{2,1,0:T(8,128)} %broadcast_9_refs_1_.2.clone.1.refs_1_), custom_call_target="tpu_custom_call", output_to_operand_aliasing={{}: (2, {})} | custom-call | tf_op jit(solution)/shard_map/pallas_call | solution.py:122
  94.1 9.6 %all-to-all-done.1 = f32[32,4,8,768]{3,2,1,0:T(8,128)} async-done(((f32[32,4,8,768]{3,2,1,0:T(8,128)}), f32[32,4,8,768]{3,2,1,0:T(8,128)}, u32[]{:S(2)}, u32[]{:S(2)}) %all-to-all-start.1) | async-done | bytes 3145760 | tf_op jit(solution)/shard_map/all_to_all | solution.py:163
  103.7 103.9 %while.21 = (s32[]{:T(128)}, f32[32,4,8,768]{3,2,1,0:T(8,128)}, f32[32,4,8,768]{3,2,0,1:T(8,128)}, f32[4,512,512]{2,1,0:T(8,128)}, f32[4,512,512]{2,1,0:T(8,128)...) while((s32[]{:T(128)}, f32[32,4,8,768]{3,2,1,0:T(8,128)}, ...), condition=%wide.region_2.3_spmd, body=%wide.region_1.2_spmd.sunk | while | flops 2419064832 | bytes 54001900 | solution.py:184
  103.7 3.9 %copy.52 = f32[32,4,8,768]{3,2,1,0:T(8,128)} copy(f32[32,4,8,768]{3,2,0,1:T(8,128)} %get-tuple-element.367) | data formatting | bytes 6291456 | tf_op jit(solution)/shard_map
  107.6 4.1 %all-to-all-start = ((f32[32,4,8,768]{3,2,1,0:T(8,128)}), f32[32,4,8,768]{3,2,1,0:T(8,128)S(1)}, u32[]{:S(2)}, u32[]{:S(2)}) async-start(f32[32,4,8,768]{3,2,1,0:T(8,128)} %copy.52), calls=%async_computation | async-start | bytes 6291456 | tf_op jit(solution)/shard_map/while/body/eval_jaxpr/all_to_all | solution.py:163
  111.7 7.3 %convolution_bitcast_fusion.7.refs_0_ = f32[4,768,512]{2,1,0:T(8,128)} fusion(f32[32,4,8,768]{3,2,1,0:T(8,128)} %get-tuple-element.366, f32[32,8,512]{2,1,0:T(8,128)} %get-tuple-element.385), kind=kOutput, calls=%fused_computation.5.clone.1 | convolution fusion | flops 2415919104 | bytes 9961472 | tf_op jit(solution)/shard_map/while/body/eval_jaxpr/asuc,auj->scj/dot_general | solution.py:166
  118.9 9.9 %eval_jaxpr.16 = f32[4,512,512]{2,1,0:T(8,128)} custom-call(s32[4]{0:T(128)S(1)} %get-tuple-element.386.offs_ref, f32[4,768,512]{2,1,0:T(8,128)} %convolution_bitcast_fusion.7.refs_0_, f32[4,512,512]{2,1,0:T(8,128)} %get-tuple-element.368.refs_1_), custom_call_target="tpu_custom_call", output_to_operand_aliasing={{}: (2, {})} | custom-call | tf_op jit(solution)/shard_map/while/body/eval_jaxpr/pallas_call | solution.py:122
  128.9 9.9 %eval_jaxpr.17 = f32[4,512,512]{2,1,0:T(8,128)} custom-call(s32[4]{0:T(128)S(1)} %get-tuple-element.387.offs_ref, f32[4,768,512]{2,1,0:T(8,128)} %convolution_bitcast_fusion.7.refs_0_, f32[4,512,512]{2,1,0:T(8,128)} %get-tuple-element.369.refs_1_), custom_call_target="tpu_custom_call", output_to_operand_aliasing={{}: (2, {})} | custom-call | tf_op jit(solution)/shard_map/while/body/eval_jaxpr/pallas_call | solution.py:122
  138.8 1.7 constant_dynamic-slice_fusion.2
  141.1 1.9 fusion.77
  143.0 11.1 %all-to-all-done = f32[32,4,8,768]{3,2,1,0:T(8,128)S(1)} async-done(((f32[32,4,8,768]{3,2,1,0:T(8,128)}), f32[32,4,8,768]{3,2,1,0:T(8,128)S(1)}, u32[]{:S(2)}, u32[]{:S(2)}) %all-to-all-start) | async-done | bytes 3145760 | tf_op jit(solution)/shard_map/while/body/eval_jaxpr/all_to_all | solution.py:163
  154.1 1.6 copy.68
  155.7 3.9 %copy.52 = f32[32,4,8,768]{3,2,1,0:T(8,128)} copy(f32[32,4,8,768]{3,2,0,1:T(8,128)} %get-tuple-element.367) | data formatting | bytes 6291456 | tf_op jit(solution)/shard_map
  159.7 4.4 %all-to-all-start = ((f32[32,4,8,768]{3,2,1,0:T(8,128)}), f32[32,4,8,768]{3,2,1,0:T(8,128)S(1)}, u32[]{:S(2)}, u32[]{:S(2)}) async-start(f32[32,4,8,768]{3,2,1,0:T(8,128)} %copy.52), calls=%async_computation | async-start | bytes 6291456 | tf_op jit(solution)/shard_map/while/body/eval_jaxpr/all_to_all | solution.py:163
  164.1 7.3 %convolution_bitcast_fusion.7.refs_0_ = f32[4,768,512]{2,1,0:T(8,128)} fusion(f32[32,4,8,768]{3,2,1,0:T(8,128)} %get-tuple-element.366, f32[32,8,512]{2,1,0:T(8,128)} %get-tuple-element.385), kind=kOutput, calls=%fused_computation.5.clone.1 | convolution fusion | flops 2415919104 | bytes 9961472 | tf_op jit(solution)/shard_map/while/body/eval_jaxpr/asuc,auj->scj/dot_general | solution.py:166
  171.4 9.9 %eval_jaxpr.16 = f32[4,512,512]{2,1,0:T(8,128)} custom-call(s32[4]{0:T(128)S(1)} %get-tuple-element.386.offs_ref, f32[4,768,512]{2,1,0:T(8,128)} %convolution_bitcast_fusion.7.refs_0_, f32[4,512,512]{2,1,0:T(8,128)} %get-tuple-element.368.refs_1_), custom_call_target="tpu_custom_call", output_to_operand_aliasing={{}: (2, {})} | custom-call | tf_op jit(solution)/shard_map/while/body/eval_jaxpr/pallas_call | solution.py:122
  181.3 9.9 %eval_jaxpr.17 = f32[4,512,512]{2,1,0:T(8,128)} custom-call(s32[4]{0:T(128)S(1)} %get-tuple-element.387.offs_ref, f32[4,768,512]{2,1,0:T(8,128)} %convolution_bitcast_fusion.7.refs_0_, f32[4,512,512]{2,1,0:T(8,128)} %get-tuple-element.369.refs_1_), custom_call_target="tpu_custom_call", output_to_operand_aliasing={{}: (2, {})} | custom-call | tf_op jit(solution)/shard_map/while/body/eval_jaxpr/pallas_call | solution.py:122
  191.2 1.7 constant_dynamic-slice_fusion.2
  193.6 1.9 fusion.77
  195.5 10.4 %all-to-all-done = f32[32,4,8,768]{3,2,1,0:T(8,128)S(1)} async-done(((f32[32,4,8,768]{3,2,1,0:T(8,128)}), f32[32,4,8,768]{3,2,1,0:T(8,128)S(1)}, u32[]{:S(2)}, u32[]{:S(2)}) %all-to-all-start) | async-done | bytes 3145760 | tf_op jit(solution)/shard_map/while/body/eval_jaxpr/all_to_all | solution.py:163
  207.5 3.5 %copy.39 = f32[32,2,8,768]{3,2,1,0:T(8,128)} copy(f32[32,2,8,768]{3,0,2,1:T(8,128)} %fusion.14) | data formatting | bytes 3145728 | tf_op jit(solution)/shard_map/optimization_barrier | solution.py:185
  211.1 5.4 %all-to-all-start.3 = ((f32[32,2,8,768]{3,2,1,0:T(8,128)}), f32[32,2,8,768]{3,2,1,0:T(8,128)}, u32[]{:S(2)}, u32[]{:S(2)}) async-start(f32[32,2,8,768]{3,2,1,0:T(8,128)} %copy.39), calls=%async_computation.3 | async-start | bytes 3145728 | tf_op jit(solution)/shard_map/all_to_all | solution.py:163
  216.6 9.2 %convolution_bitcast_fusion.1.refs_0_ = f32[4,768,512]{2,1,0:T(8,128)} fusion(f32[32,4,8,768]{3,2,1,0:T(8,128)} %get-tuple-element.221, f32[32,8,512]{2,1,0:T(8,128)S(1)} %copy-done.12), kind=kOutput, calls=%fused_computation.20 | convolution fusion | flops 2415919104 | bytes 9961472 | tf_op jit(solution)/shard_map/asuc,auj->scj/dot_general | solution.py:166
  225.8 9.9 %shard_map.39.refs_1_ = f32[4,512,512]{2,1,0:T(8,128)} custom-call(s32[4]{0:T(128)S(1)} %get-tuple-element.404, f32[4,768,512]{2,1,0:T(8,128)} %convolution_bitcast_fusion.1.refs_0_, f32[4,512,512]{2,1,0:T(8,128)} %get-tuple-element.222.refs_1_), custom_call_target="tpu_custom_call", output_to_operand_aliasing={{}: (2, {})} | custom-call | tf_op jit(solution)/shard_map/pallas_call | solution.py:122
  235.7 2.4 all-to-all-done.3
  238.1 2.9 convolution_bitcast_fusion.2.refs_0_.refs_1_
  241.1 6.7 %shard_map.40 = f32[4,512,512]{2,1,0:T(8,128)} custom-call(s32[4]{0:T(128)S(1)} %copy-done.6, f32[2,768,512]{2,1,0:T(8,128)S(1)} %convolution_bitcast_fusion.2.refs_0_.refs_1_, f32[4,512,512]{2,1,0:T(8,128)} %shard_map.39.refs_1_), custom_call_target="tpu_custom_call", output_to_operand_aliasing={{}: (2, {})} | custom-call | tf_op jit(solution)/shard_map/pallas_call | solution.py:122
  247.8 5.4 %convolution_bitcast_fusion.5 = f32[4,256,512]{2,1,0:T(8,128)} fusion(f32[4,512,512]{2,1,0:T(8,128)} %shard_map.40, f32[255,256]{0,1:T(8,128)S(1)} %copy-done.3, f32[257,256]{0,1:T(8,128)S(1)} %copy-done.2), kind=kOutput, calls=%fused_computation.25 | convolution fusion | flops 1610743808 | bytes 6815744 | tf_op jit(solution)/shard_map/kcr,rl->klc/dot_general | solution.py:194
  253.2 11.6 %shard_map.41 = f32[4,512,512]{2,1,0:T(8,128)} custom-call(s32[4]{0:T(128)S(1)} %copy-done.8, f32[4,768,512]{2,1,0:T(8,128)} %convolution_bitcast_fusion.1.refs_0_, f32[2,768,512]{2,1,0:T(8,128)S(1)} %convolution_bitcast_fusion.2.refs_0_.refs_1_, f32[4,512,512]{2,1,0:T(8,128)} %get-tuple-element.223.refs_2_), custom_call_target="tpu_custom_call", output_to_operand_aliasing={{}: (3, {})} | custom-call | tf_op jit(solution)/shard_map/pallas_call | solution.py:122
  264.8 4.2 %convolution_bitcast_fusion.4 = f32[4,256,512]{2,1,0:T(8,128)S(1)} fusion(f32[4,512,512]{2,1,0:T(8,128)} %shard_map.41, f32[255,256]{0,1:T(8,128)S(1)} %copy-done.4, f32[257,256]{0,1:T(8,128)S(1)} %copy-done.2), kind=kOutput, calls=%fused_computation.24 | convolution fusion | flops 1610743808 | bytes 6815744 | tf_op jit(solution)/shard_map/kcr,rl->klc/dot_general | solution.py:194
  269.0 44.9 %all_to_all.33 = f32[4,256,512]{2,1,0:T(8,128)S(1)} all-to-all(f32[4,256,512]{2,1,0:T(8,128)S(1)} %convolution_bitcast_fusion.4), channel_id=1, replica_groups=mesh['chan'=32,'tm'=4] {'tm'}, dimensions={0} | all-to-all | bytes 4194304 | tf_op jit(solution)/shard_map/all_to_all | solution.py:197
  314.2 2.1 pad_maximum_fusion.10
  (59 shorter events, 13.2 us)
Async XLA Ops:
  6.5 4.0 %copy-start = (f32[16,8,16384]{2,1,0:T(8,128)S(1)}, f32[16,8,16384]{2,1,0:T(8,128)}, u32[]{:S(2)}) copy-start(f32[16,8,16384]{2,1,0:T(8,128)} %param.5) | copy-start | bytes 25165828
  15.6 14.3 %copy-start.10 = (s32[8]{0:T(128)S(1)}, s32[8]{0:T(128)}, u32[]{:S(2)}) copy-start(s32[8]{0:T(128)} %param.7) | copy-start | bytes 100
  19.9 34.3 %all-to-all-start.2 = ((f32[32,2,8,768]{3,2,1,0:T(8,128)}), f32[32,2,8,768]{3,2,1,0:T(8,128)}, u32[]{:S(2)}, u32[]{:S(2)}) async-start(f32[32,2,8,768]{3,2,1,0:T(8,128)} %copy.38), calls=%async_computation.2 | async-start | bytes 3145728 | tf_op jit(solution)/shard_map/all_to_all | solution.py:163
  54.2 49.5 %all-to-all-start.1 = ((f32[32,4,8,768]{3,2,1,0:T(8,128)}), f32[32,4,8,768]{3,2,1,0:T(8,128)}, u32[]{:S(2)}, u32[]{:S(2)}) async-start(f32[32,4,8,768]{3,2,1,0:T(8,128)} %copy.37), calls=%async_computation.1 | async-start | bytes 6291456 | tf_op jit(solution)/shard_map/all_to_all | solution.py:163
  59.2 2.2 copy-start.1
  61.9 1.9 copy-start.9
  72.6 3.0 copy-start.11
  107.6 46.5 %all-to-all-start = ((f32[32,4,8,768]{3,2,1,0:T(8,128)}), f32[32,4,8,768]{3,2,1,0:T(8,128)S(1)}, u32[]{:S(2)}, u32[]{:S(2)}) async-start(f32[32,4,8,768]{3,2,1,0:T(8,128)} %copy.52), calls=%async_computation | async-start | bytes 6291456 | tf_op jit(solution)/shard_map/while/body/eval_jaxpr/all_to_all | solution.py:163
  159.7 46.2 %all-to-all-start = ((f32[32,4,8,768]{3,2,1,0:T(8,128)}), f32[32,4,8,768]{3,2,1,0:T(8,128)S(1)}, u32[]{:S(2)}, u32[]{:S(2)}) async-start(f32[32,4,8,768]{3,2,1,0:T(8,128)} %copy.52), calls=%async_computation | async-start | bytes 6291456 | tf_op jit(solution)/shard_map/while/body/eval_jaxpr/all_to_all | solution.py:163
  207.5 3.5 %copy-start.7 = (s32[4]{0:T(128)}, s32[4]{0:T(128)S(1)}, u32[]{:S(2)}) copy-start(s32[4]{0:T(128)S(1)} %get-tuple-element.405) | copy-start | bytes 52
  207.5 18.2 %copy-start.5 = (s32[4]{0:T(128)}, s32[4]{0:T(128)S(1)}, u32[]{:S(2)}) copy-start(s32[4]{0:T(128)S(1)} %get-tuple-element.404) | copy-start | bytes 52
  207.5 9.0 %copy-start.12 = (f32[32,8,512]{2,1,0:T(8,128)S(1)}, f32[32,8,512]{2,1,0:T(8,128)}, u32[]{:S(2)}) copy-start(f32[32,8,512]{2,1,0:T(8,128)} %get-tuple-element.406) | copy-start | bytes 1572868
  211.1 27.1 %all-to-all-start.3 = ((f32[32,2,8,768]{3,2,1,0:T(8,128)}), f32[32,2,8,768]{3,2,1,0:T(8,128)}, u32[]{:S(2)}, u32[]{:S(2)}) async-start(f32[32,2,8,768]{3,2,1,0:T(8,128)} %copy.39), calls=%async_computation.3 | async-start | bytes 3145728 | tf_op jit(solution)/shard_map/all_to_all | solution.py:163
  216.5 97.7 %reduce-scatter.2.cloned.1.call-start = ((), (), s32[]{:S(2)}) async-start(), calls=%async_computation.6 | async-start | bytes 2621440 | tf_op jit(solution)/shard_map/reduce_scatter | solution.py:196
  235.7 5.4 %copy-start.6 = (s32[4]{0:T(128)S(1)}, s32[4]{0:T(128)}, u32[]{:S(2)}) copy-start(s32[4]{0:T(128)} %copy-done.5) | copy-start | bytes 52
  241.1 6.7 %copy-start.2 = (f32[257,256]{0,1:T(8,128)S(1)}, f32[257,256]{0,1:T(8,128)}, u32[]{:S(2)}) copy-start(f32[257,256]{0,1:T(8,128)} %slice.184) | copy-start | bytes 789508
  241.1 6.7 %copy-start.3 = (f32[255,256]{0,1:T(8,128)S(1)}, f32[255,256]{0,1:T(8,128)}, u32[]{:S(2)}) copy-start(f32[255,256]{0,1:T(8,128)} %slice.185) | copy-start | bytes 783364
  247.8 5.4 %copy-start.8 = (s32[4]{0:T(128)S(1)}, s32[4]{0:T(128)}, u32[]{:S(2)}) copy-start(s32[4]{0:T(128)} %copy-done.7) | copy-start | bytes 52
  253.2 11.7 %copy-start.4 = (f32[255,256]{0,1:T(8,128)S(1)}, f32[255,256]{0,1:T(8,128)}, u32[]{:S(2)}) copy-start(f32[255,256]{0,1:T(8,128)} %slice.185) | copy-start | bytes 783364
Sparse Core Ops, SparseCore 0:
  253.3 53.2 reduce-scatter.1
